TPU v7x, 128 devices: a whole 4x4x4 slice. The times are simulated.
128 devices in a mesh: req: 32 (over x, z, core), tp: 4 (over y).
Axes of the slice: x: 4, y: 4, z: 4, core: 2. Of those that a mesh axis runs over, the one named last changes fastest.
Arguments:
- hidden: bfloat16 [8192, 2048], P('req', 'tp'), may hold values from -45 to 45
- routes: int32 [8192, 2], P('req'), may hold values from 0 to 7, all different within a row; in each aligned block of 256 rows (0 to 255, 256 to 511, ...) at most 128 rows name the same one
- route_weights: float32 [8192, 2], P('req'), may hold values from 0.2 to 1
- pre_gain: float32 [2048], replicated, may hold values from 0.1 to 1.9
- out_gain: float32 [2048], P('tp'), may hold values from 0.1 to 1.9
- gate_weight: bfloat16 [32, 2048, 5632], P('req', None, 'tp'), as said below
- up_weight: bfloat16 [32, 2048, 5632], P('req', None, 'tp'), as said below
- down_weight: bfloat16 [32, 5632, 2048], P('req', 'tp'), as said below
Outputs:
- residual_out: bfloat16 [8192, 2048], P('req', 'tp')
- normed_out: bfloat16 [8192, 2048], P('req', 'tp')
Inputs may be any that keep to these rules, and one draw needn't show every extreme that they name: `routes`: each row names 2 different experts; in the rows of one index of req no expert is named by more than 128 rows, a bound that some block reaches. `gate_weight`: index r holds expert r % 8. `up_weight`: index r holds expert r % 8. `down_weight`: index r holds expert r % 8.
All inputs are finite; a program needn't handle non-finite values.
Results may differ from a plain program's by a relative error of at most 0.007.
Values may be sent and summed in bfloat16 or wider, within the bound.
No kernel may reach another device: no remote copies, remote signals or barrier semaphores. Data moves between devices by JAX's collectives and lax.ppermute only.
A program may use at most 128 MiB of HBM per device.

v0:
```python
import jax
import jax.numpy as jnp
from jax import lax
from jax.sharding import PartitionSpec as P

E = 8
CAP = 128
epsilon = 1e-05


def shards(hidden, routes, route_weights, pre_gain, out_gain, gate_weight, up_weight, down_weight):
    row_count, col_part = hidden.shape
    tp_count = lax.axis_size("tp")
    req_count = lax.axis_size("req")
    full_width = col_part * tp_count
    copies = req_count // E
    slot_count = CAP // copies
    stream = hidden.astype(jnp.float32)
    whole_rows = lax.all_gather(hidden, "tp", axis=1, tiled=True).astype(jnp.float32)
    meansq = jnp.sum(whole_rows * whole_rows, axis=1) / full_width
    normed_in = (whole_rows * lax.rsqrt(meansq + epsilon)[:, None] * pre_gain[None, :]).astype(
        jnp.bfloat16
    )
    send_cols = normed_in.shape[1]
    chosen = routes.reshape(-1)
    onehot = (chosen[:, None] == jnp.arange(E, dtype=jnp.int32)[None, :]).astype(jnp.int32)
    slot_rank = jnp.sum((jnp.cumsum(onehot, axis=0) - 1) * onehot, axis=1)
    position = chosen * CAP + slot_rank
    entry_rows = jnp.arange(chosen.shape[0], dtype=jnp.int32) // routes.shape[1]
    slot_row = jnp.zeros((E * CAP,), jnp.int32).at[position].set(entry_rows)
    slot_live = jnp.zeros((E * CAP,), jnp.bool_).at[position].set(True)
    outgoing = jnp.where(slot_live[:, None], normed_in[slot_row], jnp.zeros((), jnp.bfloat16))
    outgoing = outgoing.reshape(E, slot_count, copies, send_cols).transpose(2, 0, 1, 3)
    outgoing = outgoing.reshape(req_count, slot_count, send_cols)
    pieces = lax.all_to_all(outgoing, "req", split_axis=0, concat_axis=0, tiled=True)
    sources, items, widths = pieces.shape
    flat_rows = pieces.reshape(sources * items, widths)
    gate_val = jnp.dot(flat_rows, gate_weight[0], preferred_element_type=jnp.float32)
    up_val = jnp.dot(flat_rows, up_weight[0], preferred_element_type=jnp.float32)
    activ = (jax.nn.silu(gate_val) * up_val).astype(jnp.bfloat16)
    partial_out = jnp.dot(activ, down_weight[0], preferred_element_type=jnp.float32)
    partial_out = lax.optimization_barrier(partial_out.astype(jnp.bfloat16)).astype(jnp.float32)
    summed = lax.psum_scatter(
        partial_out.reshape(sources, items, widths).astype(jnp.bfloat16),
        "tp",
        scatter_dimension=2,
        tiled=True,
    )
    returned = lax.all_to_all(summed, "req", split_axis=0, concat_axis=0, tiled=True)
    returned = returned.reshape(copies, E, slot_count, col_part).transpose(1, 2, 0, 3)
    returned = returned.reshape(E * CAP, col_part)
    picked = returned[position].reshape(row_count, routes.shape[1], col_part).astype(jnp.float32)
    mixed = jnp.sum(picked * route_weights[:, :, None], axis=1)
    total_stream = stream + mixed
    out_sums = lax.psum(jnp.sum(total_stream * total_stream, axis=1), "tp")
    normed_out = (
        total_stream * lax.rsqrt(out_sums / full_width + epsilon)[:, None] * out_gain[None, :]
    )
    return (total_stream.astype(jnp.bfloat16), normed_out.astype(jnp.bfloat16))


def solution(mesh):
    return jax.shard_map(
        shards,
        mesh=mesh,
        in_specs=(
            P("req", "tp"),
            P("req", None),
            P("req", None),
            P(),
            P("tp"),
            P("req", None, "tp"),
            P("req", None, "tp"),
            P("req", "tp", None),
        ),
        out_specs=(P("req", "tp"), P("req", "tp")),
        check_vma=False,
    )
```

profile of v0, /device:TPU:0, one launch (start us, length us, event | category | flops | bytes accessed | tf_op | source)
XLA Modules:
  0.0 241.1 jit_solution(10688515270769743538)
XLA Ops:
  7.2 0.7 all-gather.2.cloned.1.call-update
  7.9 0.8 copy.13
  8.8 0.1 eq.29
  8.9 0.1 eq.25
  9.1 1.1 reduce-window.6
  10.2 0.2 slice_reduce_fusion
  10.5 0.7 broadcast_multiply_fusion
  11.2 0.1 copy.12
  11.6 2.4 %scatter_custom_fusion.1 = s32[1024]{0:T(1024)S(1)} fusion(s32[512]{0:T(512)S(1)} %bitcast.42, s32[512]{0:T(512)S(1)} %add_select_fusion, s32[]{:T(128)} %constant.37.clone.1), kind=kCustom, calls=%fused_computation.41 | custom fusion | bytes 4100 | tf_op jit(solution)/shard_map/scatter | solution.py:30
  14.0 2.4 %scatter_custom_fusion = pred[1024]{0:T(1024)(128)(4,1)S(1)} fusion(s32[512]{0:T(512)S(1)} %bitcast.43, pred[512]{0:T(512)(128)(4,1)S(1)} %broadcast.99, pred[]{:T(512)} %constant.20.clone.1), kind=kCustom, calls=%fused_computation.44 | custom fusion | bytes 1025 | tf_op jit(solution)/shard_map/scatter | solution.py:31
  16.5 0.2 broadcast_in_dim.35
  16.8 19.4 %all-gather.2.cloned.1.call-done = bf16[256,2048]{1,0:T(8,128)(2,1)} async-done(((bf16[256,512]{1,0:T(8,128)(2,1)}), bf16[256,2048]{1,0:T(8,128)(2,1)}) %all-gather.2.cloned.1.call-update) | async-done | bytes 1048592 | tf_op jit(solution)/shard_map/all_gather | solution.py:19
  36.1 1.5 fusion.16
  37.7 1.5 fusion.18
  39.2 6.0 %gather_fusion = bf16[1024,2048]{1,0:T(8,128)(2,1)} fusion(bf16[256,2048]{1,0:T(8,128)(2,1)S(1)} %fusion.18, s32[1024]{0:T(1024)S(1)} %fusion.22), kind=kCustom, calls=%fused_computation | custom fusion | bytes 8392704 | tf_op jit(solution)/shard_map/gather | solution.py:32
  45.2 7.2 %gather.9 = bf16[8,32,4,2048]{3,2,1,0:T(4,128)(2,1)} reshape(bf16[1024,2048]{1,0:T(8,128)(2,1)} %gather_fusion) | data formatting | bytes 8388608 | tf_op jit(solution)/shard_map/gather | solution.py:32
  52.4 8.5 %copy_select_fusion = bf16[8,32,4,2048]{3,1,0,2:T(8,128)(2,1)S(1)} fusion(bf16[8,32,4,2048]{3,2,1,0:T(4,128)(2,1)} %gather.9, pred[8,32,4]{1,0,2:T(8,128)(4,1)S(1)} %copy.15), kind=kLoop, calls=%fused_computation.11 | loop fusion | flops 2097152 | bytes 8389632 | tf_op jit(solution)/shard_map/jit(_where)/select_n | solution.py:32
  60.9 57.5 %all_to_all.10 = bf16[32,32,2048]{2,1,0:T(8,128)(2,1)S(1)} all-to-all(bf16[32,32,2048]{2,1,0:T(8,128)(2,1)S(1)} %bitcast.36), channel_id=1, replica_groups=mesh['req'=32,'tp'=4] {'req'}, dimensions={0} | all-to-all | bytes 8388608 | tf_op jit(solution)/shard_map/all_to_all | solution.py:35
  118.4 2.1 copy-done
  120.5 10.2 %fusion.4 = f32[1024,1408]{1,0:T(8,128)} fusion(bf16[1024,2048]{1,0:T(8,128)(2,1)S(1)} %bitcast.38, bf16[1,2048,1408]{2,1,0:T(8,128)(2,1)} %param.13), kind=kOutput, calls=%fused_computation.8 | convolution fusion | flops 5905580032 | bytes 15728640 | tf_op jit(solution)/shard_map/dot_general | solution.py:38
  130.8 20.6 %fusion.10 = bf16[1024,2048]{1,0:T(8,128)(2,1)} fusion(bf16[1,1408,2048]{2,1,0:T(8,128)(2,1)} %param.15, f32[1024,1408]{1,0:T(8,128)} %fusion.4, bf16[1024,2048]{1,0:T(8,128)(2,1)} %bitcast.39, bf16[1,2048,1408]{2,1,0:T(8,128)(2,1)} %param.14), kind=kOutput, calls=%fused_computation.12 | convolution fusion | flops 11821907968 | bytes 25690112 | tf_op jit(solution)/shard_map/dot_general | solution.py:41
  151.4 44.1 %reduce-scatter.2.cloned.1.call-done = bf16[32,32,512]{2,1,0:T(8,128)(2,1)} async-done(((bf16[32,32,2048]{2,1,0:T(8,128)(2,1)}), bf16[32,32,512]{2,1,0:T(8,128)(2,1)}) %reduce-scatter.2.cloned.1.call-update) | async-done | bytes 1048592 | tf_op jit(solution)/shard_map/reduce_scatter | solution.py:43
  195.5 7.2 %all-to-all-start.1 = ((bf16[32,32,512]{2,1,0:T(8,128)(2,1)}), bf16[32,32,512]{2,1,0:T(8,128)(2,1)S(1)}, u32[]{:S(2)}, u32[]{:S(2)}) async-start(bf16[32,32,512]{2,1,0:T(8,128)(2,1)} %reduce-scatter.2.cloned.1.call-done), calls=%async_computation.2 | async-start | bytes 2097152 | tf_op jit(solution)/shard_map/all_to_all | solution.py:49
  202.9 16.6 %all-to-all-done.1 = bf16[32,32,512]{2,1,0:T(8,128)(2,1)S(1)} async-done(((bf16[32,32,512]{2,1,0:T(8,128)(2,1)}), bf16[32,32,512]{2,1,0:T(8,128)(2,1)S(1)}, u32[]{:S(2)}, u32[]{:S(2)}) %all-to-all-start.1) | async-done | bytes 1048608 | tf_op jit(solution)/shard_map/all_to_all | solution.py:49
  219.6 0.8 copy.21
  220.4 0.3 reshape.90
  220.7 2.0 gather_fusion.1
  222.7 0.7 reshape.91
  223.4 1.3 multiply_reduce_fusion
  224.7 0.1 multiply_reduce_fusion.1
  224.8 8.6 %psum.7 = f32[256]{0:T(256)S(1)} all-reduce(f32[256]{0:T(256)S(1)} %multiply_reduce_fusion.1), channel_id=1, replica_groups=mesh['req'=32,'tp'=4] {'tp'}, use_global_device_ids=true, to_apply=%region_9.10 | all-reduce | flops 256 | bytes 2048 | tf_op jit(solution)/shard_map/psum | solution.py:55
  233.4 0.8 multiply_convert_fusion.1
  (24 shorter events, 0.7 us)
Async XLA Ops:
  7.2 29.0 %all-gather.2.cloned.1.call-start = ((), (), s32[]{:S(2)}) async-start(), calls=%async_computation.3 | async-start | bytes 1310720 | tf_op jit(solution)/shard_map/all_gather | solution.py:19
  7.9 187.6 %reduce-scatter.2.cloned.1.call-start = ((), (), s32[]{:S(2)}) async-start(), calls=%async_computation.4 | async-start | bytes 5242880 | tf_op jit(solution)/shard_map/reduce_scatter | solution.py:43
  118.4 2.1 copy-start
  151.4 51.4 %copy-start.2 = (f32[256,2]{0,1:T(2,128)S(1)}, f32[256,2]{0,1:T(2,128)}, u32[]{:S(2)}) copy-start(f32[256,2]{0,1:T(2,128)} %param.10) | copy-start | bytes 6148
  195.5 24.1 %all-to-all-start.1 = ((bf16[32,32,512]{2,1,0:T(8,128)(2,1)}), bf16[32,32,512]{2,1,0:T(8,128)(2,1)S(1)}, u32[]{:S(2)}, u32[]{:S(2)}) async-start(bf16[32,32,512]{2,1,0:T(8,128)(2,1)} %reduce-scatter.2.cloned.1.call-done), calls=%async_computation.2 | async-start | bytes 2097152 | tf_op jit(solution)/shard_map/all_to_all | solution.py:49
  220.7 4.0 %copy-start.1 = (bf16[256,512]{1,0:T(8,128)(2,1)S(1)}, bf16[256,512]{1,0:T(8,128)(2,1)}, u32[]{:S(2)}) copy-start(bf16[256,512]{1,0:T(8,128)(2,1)} %param.8) | copy-start | bytes 786436
  220.7 12.7 %copy-start.3 = (f32[512]{0:T(512)S(1)}, f32[512]{0:T(512)}, u32[]{:S(2)}) copy-start(f32[512]{0:T(512)} %param.12) | copy-start | bytes 6148
Sparse Core Ops, SparseCore 0:
  9.7 26.4 all-gather.1
  151.5 43.9 reduce-scatter.1
where the time goes:
time: 242 us; the launch traced here: 241 us
  waiting for transfers between devices  80.8 us (33%)
  blocking collectives  66.1 us (27%)
  matrix products  30.9 us (13%)
  local copies, waits for them, and re-layouts  26 us (11%)
  other arithmetic  15.8 us (7%)
  between operations  14.2 us (6%)
  starting transfers between devices  7.31 us (3%)
    all_to_all x1, blocking collectives, shards(): lax.all_to_all(outgoing, 'req', split_axis=0, concat_axis=0, tiled=True)  57.5 us
    reduce_scatter x1, waiting for transfers between devices, shards(): lax.psum_scatter(partial_out.reshape(sources, items, widths).astype(jnp.b...  44.1 us
    dot_general x1, matrix products, shards(): jnp.dot(activ, down_weight[0], preferred_element_type=jnp.float32)  20.6 us
    all_gather x1, waiting for transfers between devices, shards(): lax.all_gather(hidden, 'tp', axis=1, tiled=True).astype(jnp.float32)  19.4 us
    all_to_all x1, waiting for transfers between devices, shards(): lax.all_to_all(summed, 'req', split_axis=0, concat_axis=0, tiled=True)  16.6 us
    gather x2, local copies, waits for them, and re-layouts, shards(): normed_in[slot_row]  13.2 us
    dot_general x1, matrix products, shards(): jnp.dot(flat_rows, gate_weight[0], preferred_element_type=jnp.float32)  10.2 us
    psum x1, blocking collectives, shards(): out_sums = lax.psum(jnp.sum(total_stream * total_stream, axis=1), 'tp')  8.58 us
  transfers between devices with their start and end apart: 3, of which 3 were waited for; matrix products, arithmetic and copies ran while one was open for 4% of the time, Pallas kernels for 0%

commit v1 on v0

--- a/solution.py
+++ b/solution.py
@@ -16,7 +16,9 @@
     copies = req_count // E
     slot_count = CAP // copies
     stream = hidden.astype(jnp.float32)
-    whole_rows = lax.all_gather(hidden, "tp", axis=1, tiled=True).astype(jnp.float32)
+    whole_rows = jnp.concatenate(
+        lax.all_to_all(jnp.stack([hidden] * lax.axis_size("tp")), "tp", 0, 0), axis=1
+    ).astype(jnp.float32)
     meansq = jnp.sum(whole_rows * whole_rows, axis=1) / full_width
     normed_in = (whole_rows * lax.rsqrt(meansq + epsilon)[:, None] * pre_gain[None, :]).astype(
         jnp.bfloat16

time: 242 us -> 232 us (0.959)
  waiting for transfers between devices: 80.8 us -> 66.2 us
  starting transfers between devices: 7.31 us -> 11.8 us
    all_gather x1 -> x0, waiting for transfers between devices: 19.4 us -> none  [shards(): lax.all_gather(hidden, 'tp', axis=1, tiled=True).astype(jnp.float32)]
    all_to_all x0 -> x1, waiting for transfers between devices: none -> 6.27 us  [shards(): lax.all_to_all(jnp.stack([hidden] * lax.axis_size('tp')), 'tp', 0, 0)]
    all_to_all x0 -> x1, starting transfers between devices: none -> 4.55 us  [shards(): lax.all_to_all(jnp.stack([hidden] * lax.axis_size('tp')), 'tp', 0, 0)]
where the time goes in v1:
time: 232 us
  blocking collectives  67.1 us (29%)
  waiting for transfers between devices  66.2 us (29%)
  matrix products  30.9 us (13%)
  local copies, waits for them, and re-layouts  28.2 us (12%)
  between operations  14.2 us (6%)
  other arithmetic  13.6 us (6%)
  starting transfers between devices  11.8 us (5%)
    all_to_all x1, blocking collectives, shards(): lax.all_to_all(outgoing, 'req', split_axis=0, concat_axis=0, tiled=True)  58.5 us
    reduce_scatter x1, waiting for transfers between devices, shards(): lax.psum_scatter(partial_out.reshape(sources, items, widths).astype(jnp.b...  43.2 us
    dot_general x1, matrix products, shards(): jnp.dot(activ, down_weight[0], preferred_element_type=jnp.float32)  20.6 us
    all_to_all x1, waiting for transfers between devices, shards(): lax.all_to_all(summed, 'req', split_axis=0, concat_axis=0, tiled=True)  16.6 us
    gather x2, local copies, waits for them, and re-layouts, shards(): normed_in[slot_row]  13.2 us
    dot_general x1, matrix products, shards(): jnp.dot(flat_rows, gate_weight[0], preferred_element_type=jnp.float32)  10.2 us
    psum x1, blocking collectives, shards(): out_sums = lax.psum(jnp.sum(total_stream * total_stream, axis=1), 'tp')  8.58 us
    select_n x1, other arithmetic, shards(): jnp.where(slot_live[:, None], normed_in[slot_row], jnp.zeros((), jnp.bflo...  8.47 us
  transfers between devices with their start and end apart: 3, of which 3 were waited for; matrix products, arithmetic and copies ran while one was open for 4% of the time, Pallas kernels for 0%

profile of v1, /device:TPU:0, one launch (start us, length us, event | category | flops | bytes accessed | tf_op | source)
XLA Modules:
  0.0 231.9 jit_solution(6911622786086220568)
XLA Ops:
  7.2 2.0 stack.2
  9.2 4.5 %all-to-all-start = ((bf16[4,256,512]{2,1,0:T(8,128)(2,1)}), bf16[4,256,512]{2,1,0:T(8,128)(2,1)S(1)}, u32[]{:S(2)}, u32[]{:S(2)}) async-start(bf16[4,256,512]{2,1,0:T(8,128)(2,1)} %stack.2), calls=%async_computation | async-start | bytes 2097152 | tf_op jit(solution)/shard_map/all_to_all | solution.py:20
  13.7 0.8 copy.20
  14.8 0.7 broadcast_multiply_fusion
  15.5 1.1 reduce-window.6
  16.7 0.2 slice_reduce_fusion
  17.3 2.4 %scatter_custom_fusion.1 = s32[1024]{0:T(1024)S(1)} fusion(s32[512]{0:T(512)S(1)} %bitcast.47, s32[512]{0:T(512)S(1)} %add_select_fusion, s32[]{:T(128)} %constant.37.clone.1), kind=kCustom, calls=%fused_computation.40 | custom fusion | bytes 4100 | tf_op jit(solution)/shard_map/scatter | solution.py:32
  19.8 2.4 %scatter_custom_fusion = pred[1024]{0:T(1024)(128)(4,1)S(1)} fusion(s32[512]{0:T(512)S(1)} %bitcast.48, pred[512]{0:T(512)(128)(4,1)S(1)} %broadcast.101, pred[]{:T(512)} %constant.20.clone.1), kind=kCustom, calls=%fused_computation.43 | custom fusion | bytes 1025 | tf_op jit(solution)/shard_map/scatter | solution.py:33
  22.2 0.2 broadcast_in_dim.35
  22.6 6.3 %all-to-all-done = bf16[4,256,512]{2,1,0:T(8,128)(2,1)S(1)} async-done(((bf16[4,256,512]{2,1,0:T(8,128)(2,1)}), bf16[4,256,512]{2,1,0:T(8,128)(2,1)S(1)}, u32[]{:S(2)}, u32[]{:S(2)}) %all-to-all-start) | async-done | bytes 1048608 | tf_op jit(solution)/shard_map/all_to_all | solution.py:20
  28.8 0.3 convert_bitcast_fusion
  29.1 0.2 copy.27
  29.4 0.3 fusion.16
  29.7 0.2 multiply_convert_fusion.1
  29.9 6.0 %gather_fusion = bf16[1024,2048]{1,0:T(8,128)(2,1)} fusion(bf16[256,2048]{1,0:T(8,128)(2,1)S(1)} %multiply_convert_fusion.1, s32[1024]{0:T(1024)S(1)} %fusion.20), kind=kCustom, calls=%fused_computation | custom fusion | bytes 8392704 | tf_op jit(solution)/shard_map/gather | solution.py:34
  35.9 7.2 %gather.9 = bf16[8,32,4,2048]{3,2,1,0:T(4,128)(2,1)} reshape(bf16[1024,2048]{1,0:T(8,128)(2,1)} %gather_fusion) | data formatting | bytes 8388608 | tf_op jit(solution)/shard_map/gather | solution.py:34
  43.1 8.5 %copy_select_fusion = bf16[8,32,4,2048]{3,1,0,2:T(8,128)(2,1)S(1)} fusion(bf16[8,32,4,2048]{3,2,1,0:T(4,128)(2,1)} %gather.9, pred[8,32,4]{1,0,2:T(8,128)(4,1)S(1)} %copy.22), kind=kLoop, calls=%fused_computation.11 | loop fusion | flops 2097152 | bytes 8389632 | tf_op jit(solution)/shard_map/jit(_where)/select_n | solution.py:34
  51.6 58.5 %all_to_all.15 = bf16[32,32,2048]{2,1,0:T(8,128)(2,1)S(1)} all-to-all(bf16[32,32,2048]{2,1,0:T(8,128)(2,1)S(1)} %bitcast.40), channel_id=1, replica_groups=mesh['req'=32,'tp'=4] {'req'}, dimensions={0} | all-to-all | bytes 8388608 | tf_op jit(solution)/shard_map/all_to_all | solution.py:37
  110.1 2.1 copy-done
  112.2 10.2 %fusion.4 = f32[1024,1408]{1,0:T(8,128)} fusion(bf16[1024,2048]{1,0:T(8,128)(2,1)S(1)} %bitcast.43, bf16[1,2048,1408]{2,1,0:T(8,128)(2,1)} %param.13), kind=kOutput, calls=%fused_computation.8 | convolution fusion | flops 5905580032 | bytes 15728640 | tf_op jit(solution)/shard_map/dot_general | solution.py:40
  122.4 20.6 %fusion.10 = bf16[1024,2048]{1,0:T(8,128)(2,1)} fusion(bf16[1,1408,2048]{2,1,0:T(8,128)(2,1)} %param.15, f32[1024,1408]{1,0:T(8,128)} %fusion.4, bf16[1024,2048]{1,0:T(8,128)(2,1)} %bitcast.44, bf16[1,2048,1408]{2,1,0:T(8,128)(2,1)} %param.14), kind=kOutput, calls=%fused_computation.12 | convolution fusion | flops 11821907968 | bytes 25690112 | tf_op jit(solution)/shard_map/dot_general | solution.py:43
  143.1 43.2 %reduce-scatter.2.cloned.1.call-done = bf16[32,32,512]{2,1,0:T(8,128)(2,1)} async-done(((bf16[32,32,2048]{2,1,0:T(8,128)(2,1)}), bf16[32,32,512]{2,1,0:T(8,128)(2,1)}) %reduce-scatter.2.cloned.1.call-update) | async-done | bytes 1048592 | tf_op jit(solution)/shard_map/reduce_scatter | solution.py:45
  186.3 7.2 %all-to-all-start.2 = ((bf16[32,32,512]{2,1,0:T(8,128)(2,1)}), bf16[32,32,512]{2,1,0:T(8,128)(2,1)S(1)}, u32[]{:S(2)}, u32[]{:S(2)}) async-start(bf16[32,32,512]{2,1,0:T(8,128)(2,1)} %reduce-scatter.2.cloned.1.call-done), calls=%async_computation.3 | async-start | bytes 2097152 | tf_op jit(solution)/shard_map/all_to_all | solution.py:51
  193.7 16.6 %all-to-all-done.2 = bf16[32,32,512]{2,1,0:T(8,128)(2,1)S(1)} async-done(((bf16[32,32,512]{2,1,0:T(8,128)(2,1)}), bf16[32,32,512]{2,1,0:T(8,128)(2,1)S(1)}, u32[]{:S(2)}, u32[]{:S(2)}) %all-to-all-start.2) | async-done | bytes 1048608 | tf_op jit(solution)/shard_map/all_to_all | solution.py:51
  210.4 0.8 copy.30
  211.2 0.3 reshape.96
  211.5 2.0 gather_fusion.1
  213.5 0.7 reshape.98
  214.1 1.3 multiply_reduce_fusion
  215.5 0.1 multiply_reduce_fusion.1
  215.6 8.6 %psum.7 = f32[256]{0:T(256)S(1)} all-reduce(f32[256]{0:T(256)S(1)} %multiply_reduce_fusion.1), channel_id=1, replica_groups=mesh['req'=32,'tp'=4] {'tp'}, use_global_device_ids=true, to_apply=%region_9.10 | all-reduce | flops 256 | bytes 2048 | tf_op jit(solution)/shard_map/psum | solution.py:57
  224.2 0.8 multiply_convert_fusion.2
  (28 shorter events, 1.1 us)
Async XLA Ops:
  9.2 19.6 %all-to-all-start = ((bf16[4,256,512]{2,1,0:T(8,128)(2,1)}), bf16[4,256,512]{2,1,0:T(8,128)(2,1)S(1)}, u32[]{:S(2)}, u32[]{:S(2)}) async-start(bf16[4,256,512]{2,1,0:T(8,128)(2,1)} %stack.2), calls=%async_computation | async-start | bytes 2097152 | tf_op jit(solution)/shard_map/all_to_all | solution.py:20
  13.7 172.6 %reduce-scatter.2.cloned.1.call-start = ((), (), s32[]{:S(2)}) async-start(), calls=%async_computation.4 | async-start | bytes 5242880 | tf_op jit(solution)/shard_map/reduce_scatter | solution.py:45
  22.5 7.1 %copy-start.2 = (f32[2048]{0:T(1024)S(1)}, f32[2048]{0:T(1024)}, u32[]{:S(2)}) copy-start(f32[2048]{0:T(1024)} %param.11) | copy-start | bytes 24580
  110.1 2.1 copy-start
  143.0 50.5 %copy-start.3 = (f32[256,2]{0,1:T(2,128)S(1)}, f32[256,2]{0,1:T(2,128)}, u32[]{:S(2)}) copy-start(f32[256,2]{0,1:T(2,128)} %param.10) | copy-start | bytes 6148
  186.3 24.0 %all-to-all-start.2 = ((bf16[32,32,512]{2,1,0:T(8,128)(2,1)}), bf16[32,32,512]{2,1,0:T(8,128)(2,1)S(1)}, u32[]{:S(2)}, u32[]{:S(2)}) async-start(bf16[32,32,512]{2,1,0:T(8,128)(2,1)} %reduce-scatter.2.cloned.1.call-done), calls=%async_computation.3 | async-start | bytes 2097152 | tf_op jit(solution)/shard_map/all_to_all | solution.py:51
  211.5 4.0 %copy-start.1 = (bf16[256,512]{1,0:T(8,128)(2,1)S(1)}, bf16[256,512]{1,0:T(8,128)(2,1)}, u32[]{:S(2)}) copy-start(bf16[256,512]{1,0:T(8,128)(2,1)} %param.8) | copy-start | bytes 786436
  211.5 12.7 %copy-start.4 = (f32[512]{0:T(512)S(1)}, f32[512]{0:T(512)}, u32[]{:S(2)}) copy-start(f32[512]{0:T(512)} %param.12) | copy-start | bytes 6148
Sparse Core Ops, SparseCore 0:
  143.2 43.0 reduce-scatter.1
